TPU v7x, 256 devices: a whole 4x4x8 slice. The times are simulated.
256 devices in a mesh: row: 8 (over y, core), col: 8 (over z_hi, x), page: 4 (over z_lo).
Axes of the slice: x: 4, y: 4, z: 8 (z_hi: 2, z_lo: 4; z = z_hi * 4 + z_lo), core: 2. Of those that a mesh axis runs over, the one named last changes fastest.
Arguments:
- tokens: bfloat16 [32, 512, 2048], P(('row', 'page'), None, 'col'), may hold values from -6 to 6
- lengths: int32 [32], P(('row', 'page')), may hold values from 1 to 512, 4096 in all
- page_slot: int32 [32, 4], P('row'), may hold values from 0 to 15, as said below
- w_query: float32 [2048, 1024], P(('row', 'page'), 'col'), may hold values from -0.125 to 0.125
- w_keyval: float32 [2, 2048, 256], P(None, ('row', 'page')), may hold values from -0.125 to 0.125
- w_out: float32 [1024, 2048], P('col', ('row', 'page')), may hold values from -0.1875 to 0.1875
- w_gateup: float32 [2, 2048, 5120], P(None, ('row', 'page'), 'col'), may hold values from -0.125 to 0.125
- w_down: float32 [5120, 2048], P('col', ('row', 'page')), may hold values from -0.078125 to 0.078125
- attn_gain: float32 [2048], replicated, may hold values from 0.1 to 1.9
- ffn_gain: float32 [2048], replicated, may hold values from 0.1 to 1.9
- query_gain: float32 [64], replicated, may hold values from 0.1 to 1.9
- key_gain: float32 [64], replicated, may hold values from 0.1 to 1.9
Outputs:
- layer_out: bfloat16 [32, 512, 2048], P(('row', 'page'), None, 'col')
- kv_pages: bfloat16 [2, 128, 128, 1024], P(None, ('row', 'page'), None, 'col')
Inputs may be any that keep to these rules, and one draw needn't show every extreme that they name: `lengths`: each prompt's real tokens; in every draw some prompt has exactly 512. `page_slot`: within the prompts of one index of row the values are a permutation; page v belongs to index v // 4 of page; the 4 blocks of the prompts of one device send the same number of blocks to each of the 4 indices of page.
All inputs are finite; a program needn't handle non-finite values. No bound on the sum of `lengths` on one device may be relied on, other than what follows from the above.
Results may differ from a plain program's by a relative error of at most 0.012.
Values may be sent and summed in bfloat16 or wider, within the bound.
No kernel may reach another device: no remote copies, remote signals or barrier semaphores. Data moves between devices by JAX's collectives and lax.ppermute only.
A program may use at most 64 MiB of HBM per device.

v0:
```python
import jax
import jax.numpy as jnp
from jax import lax
from jax.sharding import PartitionSpec as P

PAGE_LEN = 128


def normalize(values, norm_gain):
    mean_sq = jnp.mean(values * values, axis=-1, keepdims=True)
    return values * lax.rsqrt(mean_sq + 1e-06) * norm_gain


def rotate(values):
    row_count = values.shape[-3]
    head_dim = values.shape[-1]
    half_dim = head_dim // 2
    frequency = 10000.0 ** (-2.0 * jnp.arange(half_dim, dtype=jnp.float32) / head_dim)
    angles = jnp.arange(row_count, dtype=jnp.float32)[:, None] * frequency[None, :]
    cosine = jnp.cos(angles)[:, None, :]
    sine_table = jnp.sin(angles)[:, None, :]
    leading = values[..., :half_dim]
    trailing = values[..., half_dim:]
    return jnp.concatenate(
        [leading * cosine - trailing * sine_table, trailing * cosine + leading * sine_table],
        axis=-1,
    )


def attend(query_rows, key_rows, value_rows, length):
    row_count = query_rows.shape[0]
    scores = jnp.einsum(
        "qhd,khd->hqk", query_rows, key_rows, preferred_element_type=jnp.float32
    ) * query_rows.shape[2] ** (-0.5)
    positions = jnp.arange(row_count, dtype=jnp.int32)
    seen_keys = (positions[None, :] <= positions[:, None]) & (positions[None, :] < length)
    exp_scores = jnp.where(seen_keys[None], jnp.exp(scores), 0.0)
    attn_probs = (exp_scores / jnp.sum(exp_scores, axis=-1, keepdims=True)).astype(jnp.bfloat16)
    attended = jnp.einsum(
        "hqk,khd->qhd", attn_probs, value_rows, preferred_element_type=jnp.float32
    )
    live_rows = (positions < length)[:, None, None]
    return jnp.where(live_rows, attended, 0.0).astype(jnp.bfloat16)


def on_device(
    tokens,
    lengths,
    page_slot,
    w_query,
    w_keyval,
    w_out,
    w_gateup,
    w_down,
    attn_gain,
    ffn_gain,
    query_gain,
    key_gain,
):
    col_count = lax.axis_size("col")
    col_index = lax.axis_index("col")
    head_dim = query_gain.shape[0]
    local_width = w_query.shape[1]
    local_heads = local_width // head_dim
    kv_heads = w_keyval.shape[2] // head_dim
    group_size = local_heads * col_count // kv_heads
    kv_index = (col_index * local_heads + jnp.arange(local_heads, dtype=jnp.int32)) // group_size
    columns = (
        kv_index[:, None] * head_dim + jnp.arange(head_dim, dtype=jnp.int32)[None, :]
    ).reshape(-1)
    keyval_piece = w_keyval.astype(jnp.bfloat16)
    query_piece = w_query.astype(jnp.bfloat16)
    out_piece = w_out.astype(jnp.bfloat16)
    gateup_piece = w_gateup.astype(jnp.bfloat16)
    down_piece = w_down.astype(jnp.bfloat16)
    query_full, keyval_full, out_full, gateup_full, down_full = (
        lax.all_gather(query_piece, ("row", "page"), axis=0, tiled=True),
        lax.all_gather(keyval_piece, ("row", "page"), axis=1, tiled=True),
        lax.all_gather(out_piece, ("row", "page"), axis=1, tiled=True),
        lax.all_gather(gateup_piece, ("row", "page"), axis=1, tiled=True),
        lax.all_gather(down_piece, ("row", "page"), axis=1, tiled=True),
    )
    keyval_used = jnp.take(keyval_full, columns, axis=2)
    merged_qkv = jnp.concatenate([query_full, keyval_used[0], keyval_used[1]], axis=1)
    merged_gateup = jnp.concatenate([gateup_full[0], gateup_full[1]], axis=1)
    prompt_count, seq_len, local_feat = tokens.shape
    gathered = lax.all_gather(tokens, "col", axis=2, tiled=True)
    model_width = gathered.shape[2]
    attn_in = normalize(gathered.astype(jnp.float32), attn_gain).astype(jnp.bfloat16)
    projected = jnp.dot(
        attn_in.reshape(-1, model_width), merged_qkv, preferred_element_type=jnp.float32
    )
    projected = projected.reshape(prompt_count, seq_len, 3, local_heads, head_dim)
    queries = rotate(normalize(projected[:, :, 0], query_gain)).astype(jnp.bfloat16)
    keys_rot = rotate(normalize(projected[:, :, 1], key_gain)).astype(jnp.bfloat16)
    values_in = projected[:, :, 2].astype(jnp.bfloat16)
    attended_one = attend(queries[0], keys_rot[0], values_in[0], lengths[0])
    outputs = [attended_one.reshape(seq_len, local_width)]
    attended = jnp.stack(outputs)
    attn_terms = jnp.dot(
        attended.reshape(-1, local_width), out_full, preferred_element_type=jnp.float32
    )
    attn_terms = attn_terms.reshape(prompt_count, seq_len, model_width)
    attn_sum = lax.psum_scatter(
        attn_terms.astype(jnp.bfloat16), "col", scatter_dimension=2, tiled=True
    ).astype(jnp.float32)
    residual = (tokens.astype(jnp.float32) + attn_sum).astype(jnp.bfloat16)
    residual_all = lax.all_gather(residual, "col", axis=2, tiled=True)
    ffn_in = normalize(residual_all.astype(jnp.float32), ffn_gain).astype(jnp.bfloat16)
    gate_up = jnp.dot(
        ffn_in.reshape(-1, model_width), merged_gateup, preferred_element_type=jnp.float32
    )
    unit_count = gateup_full.shape[2]
    hidden = (jax.nn.silu(gate_up[:, :unit_count]) * gate_up[:, unit_count:]).astype(jnp.bfloat16)
    ffn_terms = jnp.dot(hidden, down_full, preferred_element_type=jnp.float32).reshape(
        prompt_count, seq_len, model_width
    )
    ffn_sum = lax.psum_scatter(
        ffn_terms.astype(jnp.bfloat16), "col", scatter_dimension=2, tiled=True
    ).astype(jnp.float32)
    layer_out = (residual.astype(jnp.float32) + ffn_sum).astype(jnp.bfloat16)
    page_count = lax.axis_size("page")
    page_index = lax.axis_index("page")
    blocks_each = prompt_count * (seq_len // PAGE_LEN)
    capacity = blocks_each // page_count
    owners = page_slot // blocks_each
    local_slot = page_slot % blocks_each
    same_owner = owners[:, :, None] == owners[:, None, :]
    earlier = (
        jnp.arange(blocks_each, dtype=jnp.int32)[None, :]
        < jnp.arange(blocks_each, dtype=jnp.int32)[:, None]
    )
    order_in = jnp.sum((same_owner & earlier[None]).astype(jnp.int32), axis=2)
    my_owners = lax.dynamic_index_in_dim(owners, page_index, 0, keepdims=False)
    my_order = lax.dynamic_index_in_dim(order_in, page_index, 0, keepdims=False)
    send_pos = my_owners * capacity + my_order
    live_rows = (jnp.arange(seq_len, dtype=jnp.int32)[None, :] < lengths[:, None])[:, :, None, None]
    page_keys = jnp.where(live_rows, keys_rot, jnp.zeros_like(keys_rot)).reshape(
        blocks_each, PAGE_LEN, local_width
    )
    page_values = jnp.where(live_rows, values_in, jnp.zeros_like(values_in)).reshape(
        blocks_each, PAGE_LEN, local_width
    )
    stacked = jnp.stack([page_keys, page_values])
    outgoing = jnp.zeros_like(stacked).at[:, send_pos].set(stacked)
    incoming = lax.all_to_all(outgoing, "page", split_axis=1, concat_axis=1, tiled=True)
    arrival_hit = (owners[:, None, :] == page_index) & (
        order_in[:, None, :] == jnp.arange(capacity, dtype=jnp.int32)[None, :, None]
    )
    arrival_slot = jnp.sum(jnp.where(arrival_hit, local_slot[:, None, :], 0), axis=2).reshape(
        blocks_each
    )
    kv_pages = jnp.zeros_like(incoming).at[:, arrival_slot].set(incoming)
    return (layer_out, kv_pages)


def solution(mesh):
    in_specs = (
        P(("row", "page"), None, "col"),
        P(("row", "page")),
        P("row", None),
        P(("row", "page"), "col"),
        P(None, ("row", "page"), None),
        P("col", ("row", "page")),
        P(None, ("row", "page"), "col"),
        P("col", ("row", "page")),
        P(),
        P(),
        P(),
        P(),
    )
    out_specs = (P(("row", "page"), None, "col"), P(None, ("row", "page"), None, "col"))
    return jax.shard_map(
        on_device, mesh=mesh, in_specs=in_specs, out_specs=out_specs, check_vma=False
    )
```

profile of v0, /device:TPU:8, one launch (start us, length us, event | category | flops | bytes accessed | tf_op | source)
XLA Modules:
  0.0 662.8 jit_solution(14260095701070087263)
XLA Ops:
  7.2 0.7 all-gather.6.cloned.1.call-update
  7.9 1.6 copy.63
  9.9 0.8 convert_element_type.114
  11.3 0.8 convert_element_type.121
  12.2 0.3 fusion.42
  12.5 0.8 fusion.28
  13.3 82.1 %all_gather.22 = bf16[2048,128]{1,0:T(8,128)(2,1)} all-gather(bf16[64,128]{1,0:T(8,128)(2,1)S(1)} %convert_element_type.114), channel_id=1, replica_groups=mesh['row'=8,'col'=8,'page'=4] {'row','page'}, dimensions={0}, use_global_device_ids=true | all-gather | bytes 540672 | tf_op jit(solution)/shard_map/all_gather | solution.py:77
  95.5 68.6 %all_gather.24 = bf16[128,2048]{0,1:T(8,128)(2,1)} all-gather(bf16[128,64]{0,1:T(8,128)(2,1)S(1)} %convert_element_type.121), channel_id=1, replica_groups=mesh['row'=8,'col'=8,'page'=4] {'row','page'}, dimensions={1}, use_global_device_ids=true | all-gather | bytes 540672 | tf_op jit(solution)/shard_map/all_gather | solution.py:79
  164.1 2.1 fusion.4
  166.2 9.9 %all-gather.8.cloned.1.call-done = bf16[2,2048,256]{2,0,1:T(2,128)(2,1)} async-done(((bf16[2,64,256]{2,0,1:T(2,128)(2,1)}), bf16[2,2048,256]{2,0,1:T(2,128)(2,1)}) %all-gather.8.cloned.1.call-update) | async-done | bytes 2097168 | tf_op jit(solution)/shard_map/all_gather | solution.py:78
  176.1 7.6 %copy.52 = bf16[2,2048,256]{1,0,2:T(2,128)(2,1)S(1)} copy(bf16[2,2048,256]{2,0,1:T(2,128)(2,1)} %all-gather.8.cloned.1.call-done) | data formatting | bytes 4194304 | tf_op jit(solution)/shard_map/all_gather | solution.py:78
  183.6 2.7 gather_fusion
  186.3 1.0 fusion.27
  187.3 1.5 fusion.55
  188.8 0.9 copy.53
  189.7 0.9 copy.54
  190.6 0.2 maximum_bitcast_fusion
  190.8 1.7 copy.55
  192.5 3.1 fusion.23
  196.0 0.6 copy-done.11
  196.6 0.8 fusion.21
  197.4 0.7 fusion.26
  198.1 0.3 copy-done.2
  198.4 2.1 fusion.11
  200.6 0.7 convert_element_type.129
  201.4 98.7 %reduce-scatter.3.cloned.1.call-done = bf16[1,512,256]{2,1,0:T(8,128)(2,1)} async-done(((bf16[1,512,2048]{2,1,0:T(8,128)(2,1)}), bf16[1,512,256]{2,1,0:T(8,128)(2,1)}) %reduce-scatter.3.cloned.1.call-update) | async-done | bytes 262160 | tf_op jit(solution)/shard_map/reduce_scatter | solution.py:104
  300.1 1.7 add_convert_fusion.1
  301.9 0.6 convert_element_type.131
  302.6 0.2 reduce-scatter.5.cloned.1.call-start
  302.8 85.4 %all-gather.12.cloned.1.call-done = bf16[2,2048,640]{2,1,0:T(8,128)(2,1)} async-done(((bf16[2,64,640]{2,1,0:T(8,128)(2,1)}), bf16[2,2048,640]{2,1,0:T(8,128)(2,1)}) %all-gather.12.cloned.1.call-update) | async-done | bytes 5242896 | tf_op jit(solution)/shard_map/all_gather | solution.py:80
  388.2 4.6 slice_bitcast_fusion.1
  392.8 75.0 %all-gather.10.cloned.1.call-done = bf16[1,512,2048]{2,1,0:T(8,128)(2,1)} async-done(((bf16[1,512,256]{2,1,0:T(8,128)(2,1)}), bf16[1,512,2048]{2,1,0:T(8,128)(2,1)}) %all-gather.10.cloned.1.call-update) | async-done | bytes 2097168 | tf_op jit(solution)/shard_map/all_gather | solution.py:108
  467.8 2.2 fusion.7
  470.0 6.2 fusion
  476.2 76.6 %all-gather.14.cloned.1.call-done = bf16[640,2048]{0,1:T(8,128)(2,1)} async-done(((bf16[640,64]{0,1:T(8,128)(2,1)}), bf16[640,2048]{0,1:T(8,128)(2,1)}) %all-gather.14.cloned.1.call-update) | async-done | bytes 2621456 | tf_op jit(solution)/shard_map/all_gather | solution.py:81
  552.8 5.7 fusion.10
  558.6 0.6 copy-done.13
  559.2 0.2 convert_reduce_fusion
  559.6 0.1 copy.57
  559.8 0.1 copy.58
  559.9 0.1 broadcast_select_fusion.2
  560.1 0.8 scatter_fusion
  560.9 0.7 copy.59
  561.6 4.6 all-to-all-start
  566.4 14.3 %all-to-all-done = bf16[2,4,128,128]{3,2,0,1:T(8,128)(2,1)S(1)} async-done(((bf16[2,4,128,128]{3,2,0,1:T(8,128)(2,1)}), bf16[2,4,128,128]{3,2,0,1:T(8,128)(2,1)S(1)}, u32[]{:S(2)}, u32[]{:S(2)}) %all-to-all-start) | async-done | bytes 262176 | tf_op jit(solution)/shard_map/all_to_all | solution.py:146
  580.7 0.8 scatter_fusion.1
  581.5 72.7 %reduce-scatter.5.cloned.1.call-done = bf16[1,512,256]{2,1,0:T(8,128)(2,1)} async-done(((bf16[1,512,2048]{2,1,0:T(8,128)(2,1)}), bf16[1,512,256]{2,1,0:T(8,128)(2,1)}) %reduce-scatter.5.cloned.1.call-update) | async-done | bytes 262160 | tf_op jit(solution)/shard_map/reduce_scatter | solution.py:118
  654.2 1.7 add_convert_fusion
  (74 shorter events, 1.3 us)
Async XLA Ops:
  7.2 156.9 %all-gather.6.cloned.1.call-start = ((), (), s32[]{:S(2)}) async-start(), calls=%async_computation.3 | async-start | bytes 2359296 | tf_op jit(solution)/shard_map/all_gather | solution.py:87
  7.9 168.2 %all-gather.8.cloned.1.call-start = ((), (), s32[]{:S(2)}) async-start(), calls=%async_computation.4 | async-start | bytes 2162688 | tf_op jit(solution)/shard_map/all_gather | solution.py:78
  9.6 290.5 %reduce-scatter.3.cloned.1.call-start = ((), (), s32[]{:S(2)}) async-start(), calls=%async_computation.5 | async-start | bytes 2359296 | tf_op jit(solution)/shard_map/reduce_scatter | solution.py:104
  188.8 1.7 copy-start.3
  190.8 1.7 copy-start.16
  192.5 3.3 copy-start.14
  192.5 3.3 copy-start.15
  195.6 1.0 copy-start.11
  195.9 1.4 copy-start.7
  196.0 1.4 copy-start.9
  197.4 1.0 copy-start.2
  198.4 2.2 copy-start.6
  198.4 101.7 %copy-start.4 = (bf16[1,512,256]{2,1,0:T(8,128)(2,1)S(1)}, bf16[1,512,256]{2,1,0:T(8,128)(2,1)}, u32[]{:S(2)}) copy-start(bf16[1,512,256]{2,1,0:T(8,128)(2,1)} %param.12) | copy-start | bytes 786436
  200.5 101.4 %copy-start.12 = (f32[640,64]{0,1:T(8,128)S(1)}, f32[640,64]{0,1:T(8,128)}, u32[]{:S(2)}) copy-start(f32[640,64]{0,1:T(8,128)} %param.19) | copy-start | bytes 491524
  200.5 187.7 %all-gather.12.cloned.1.call-start = ((), (), s32[]{:S(2)}) async-start(), calls=%async_computation.7 | async-start | bytes 5406720 | tf_op jit(solution)/shard_map/all_gather | solution.py:80
  201.3 266.4 %all-gather.10.cloned.1.call-start = ((), (), s32[]{:S(2)}) async-start(), calls=%async_computation.6 | async-start | bytes 2359296 | tf_op jit(solution)/shard_map/all_gather | solution.py:108
  301.8 251.0 %all-gather.14.cloned.1.call-start = ((), (), s32[]{:S(2)}) async-start(), calls=%async_computation.8 | async-start | bytes 2703360 | tf_op jit(solution)/shard_map/all_gather | solution.py:81
  302.6 351.6 %reduce-scatter.5.cloned.1.call-start = ((), (), s32[]{:S(2)}) async-start(), calls=%async_computation.9 | async-start | bytes 2359296 | tf_op jit(solution)/shard_map/reduce_scatter | solution.py:118
  392.8 77.2 %copy-start.17 = (f32[2048]{0:T(1024)S(1)}, f32[2048]{0:T(1024)}, u32[]{:S(2)}) copy-start(f32[2048]{0:T(1024)} %param.21) | copy-start | bytes 24580
  467.8 2.2 copy-start.1
  558.5 0.7 copy-start.13
  558.5 1.0 copy-start.8
  558.5 1.0 copy-start.10
  559.9 94.3 %copy-start = (bf16[1,512,256]{2,1,0:T(8,128)(2,1)S(1)}, bf16[1,512,256]{2,1,0:T(8,128)(2,1)}, u32[]{:S(2)}) copy-start(bf16[1,512,256]{2,1,0:T(8,128)(2,1)} %add_convert_fusion.1) | copy-start | bytes 786436
  561.6 19.1 %all-to-all-start = ((bf16[2,4,128,128]{3,2,0,1:T(8,128)(2,1)}), bf16[2,4,128,128]{3,2,0,1:T(8,128)(2,1)S(1)}, u32[]{:S(2)}, u32[]{:S(2)}) async-start(bf16[2,4,128,128]{3,2,0,1:T(8,128)(2,1)} %copy.59), calls=%async_computation.2 | async-start | bytes 524288 | tf_op jit(solution)/shard_map/all_to_all | solution.py:146
  581.5 74.4 %copy-start.5 = (bf16[2,4,128,128]{3,2,1,0:T(8,128)(2,1)}, bf16[2,4,128,128]{3,2,1,0:T(8,128)(2,1)S(1)}, u32[]{:S(2)}) copy-start(bf16[2,4,128,128]{3,2,1,0:T(8,128)(2,1)S(1)} %scatter_fusion.1) | copy-start | bytes 786436
Sparse Core Ops, SparseCore 0:
  10.4 74.3 all-gather.5
  87.2 88.8 all-gather.7
  200.7 99.3 reduce-scatter.2
  302.3 85.8 all-gather.11
  391.1 76.6 all-gather.9
  469.4 83.3 all-gather.13
  558.7 95.4 reduce-scatter.4
where the time goes:
time: 663 us
  waiting for transfers between devices  433 us (65%)
  blocking collectives  151 us (23%)
  local copies, waits for them, and re-layouts  25.8 us (4%)
  matrix products  18.6 us (3%)
  between operations  15.2 us (2%)
  other arithmetic  13.9 us (2%)
    reduce_scatter x1, waiting for transfers between devices, on_device(): lax.psum_scatter(attn_terms.astype(jnp.bfloat16), 'col', scatter_dimensio...  98.7 us
    all_gather x1, waiting for transfers between devices, on_device(): lax.all_gather(gateup_piece, ('row', 'page'), axis=1, tiled=True)  85.4 us
    all_gather x1, blocking collectives, on_device(): lax.all_gather(query_piece, ('row', 'page'), axis=0, tiled=True)  82.1 us
    all_gather x1, waiting for transfers between devices, on_device(): lax.all_gather(down_piece, ('row', 'page'), axis=1, tiled=True)  76.6 us
    all_gather x1, waiting for transfers between devices, on_device(): residual_all = lax.all_gather(residual, 'col', axis=2, tiled=True)  75 us
    reduce_scatter x1, waiting for transfers between devices, on_device(): lax.psum_scatter(ffn_terms.astype(jnp.bfloat16), 'col', scatter_dimension...  72.7 us
    all_gather x1, blocking collectives, on_device(): lax.all_gather(out_piece, ('row', 'page'), axis=1, tiled=True)  68.6 us
    all_to_all x1, waiting for transfers between devices, on_device(): lax.all_to_all(outgoing, 'page', split_axis=1, concat_axis=1, tiled=True)  14.3 us
  transfers between devices with their start and end apart: 8, of which 7 were waited for; matrix products, arithmetic and copies ran while one was open for 4% of the time, Pallas kernels for 0%

commit v1 on v0

--- a/solution.py
+++ b/solution.py
@@ -105,7 +105,9 @@
         attn_terms.astype(jnp.bfloat16), "col", scatter_dimension=2, tiled=True
     ).astype(jnp.float32)
     residual = (tokens.astype(jnp.float32) + attn_sum).astype(jnp.bfloat16)
-    residual_all = lax.all_gather(residual, "col", axis=2, tiled=True)
+    residual_all = jnp.concatenate(
+        lax.all_to_all(jnp.stack([residual] * lax.axis_size("col")), "col", 0, 0), axis=2
+    )
     ffn_in = normalize(residual_all.astype(jnp.float32), ffn_gain).astype(jnp.bfloat16)
     gate_up = jnp.dot(
         ffn_in.reshape(-1, model_width), merged_gateup, preferred_element_type=jnp.float32

time: 663 us -> 624 us (0.941)
  waiting for transfers between devices: 433 us -> 388 us
    all_gather x1 -> x0, waiting for transfers between devices: 75 us -> none  [on_device(): residual_all = lax.all_gather(residual, 'col', axis=2, tiled=True)]
    all_gather x1, waiting for transfers between devices: 85.4 us -> 113 us  [on_device(): lax.all_gather(gateup_piece, ('row', 'page'), axis=1, tiled=True)]
  transfers between devices with their start and end apart: 8 -> 8, of which waited for: 7 -> 6; matrix products, arithmetic and copies ran while one was open for 4% -> 4% of each run, Pallas kernels for 0% -> 0%
where the time goes in v1:
time: 624 us
  waiting for transfers between devices  388 us (62%)
  blocking collectives  151 us (24%)
  local copies, waits for them, and re-layouts  30.4 us (5%)
  matrix products  16.9 us (3%)
  between operations  15.1 us (2%)
  other arithmetic  13.5 us (2%)
  starting transfers between devices  8.72 us (1%)
    all_gather x1, waiting for transfers between devices, on_device(): lax.all_gather(gateup_piece, ('row', 'page'), axis=1, tiled=True)  113 us
    reduce_scatter x1, waiting for transfers between devices, on_device(): lax.psum_scatter(attn_terms.astype(jnp.bfloat16), 'col', scatter_dimensio...  98.9 us
    all_gather x1, blocking collectives, on_device(): lax.all_gather(query_piece, ('row', 'page'), axis=0, tiled=True)  82.1 us
    all_gather x1, waiting for transfers between devices, on_device(): lax.all_gather(down_piece, ('row', 'page'), axis=1, tiled=True)  78.6 us
    reduce_scatter x1, waiting for transfers between devices, on_device(): lax.psum_scatter(ffn_terms.astype(jnp.bfloat16), 'col', scatter_dimension...  72.5 us
    all_gather x1, blocking collectives, on_device(): lax.all_gather(out_piece, ('row', 'page'), axis=1, tiled=True)  68.6 us
    all_to_all x1, waiting for transfers between devices, on_device(): lax.all_to_all(outgoing, 'page', split_axis=1, concat_axis=1, tiled=True)  14.3 us
  transfers between devices with their start and end apart: 8, of which 6 were waited for; matrix products, arithmetic and copies ran while one was open for 4% of the time, Pallas kernels for 0%

profile of v1, /device:TPU:8, one launch (start us, length us, event | category | flops | bytes accessed | tf_op | source)
XLA Modules:
  0.0 623.6 jit_solution(9426843928234597706)
XLA Ops:
  7.2 0.7 all-gather.5.cloned.1.call-update
  7.9 1.6 copy.70
  9.9 0.8 convert_element_type.133
  11.3 0.8 convert_element_type.140
  12.2 0.3 fusion.38
  12.5 0.8 fusion.23
  13.3 82.1 %all_gather.19 = bf16[2048,128]{1,0:T(8,128)(2,1)} all-gather(bf16[64,128]{1,0:T(8,128)(2,1)S(1)} %convert_element_type.133), channel_id=1, replica_groups=mesh['row'=8,'col'=8,'page'=4] {'row','page'}, dimensions={0}, use_global_device_ids=true | all-gather | bytes 540672 | tf_op jit(solution)/shard_map/all_gather | solution.py:77
  95.5 68.6 %all_gather.21 = bf16[128,2048]{0,1:T(8,128)(2,1)} all-gather(bf16[128,64]{0,1:T(8,128)(2,1)S(1)} %convert_element_type.140), channel_id=1, replica_groups=mesh['row'=8,'col'=8,'page'=4] {'row','page'}, dimensions={1}, use_global_device_ids=true | all-gather | bytes 540672 | tf_op jit(solution)/shard_map/all_gather | solution.py:79
  164.1 2.1 fusion.4
  166.2 9.9 %all-gather.7.cloned.1.call-done = bf16[2,2048,256]{2,0,1:T(2,128)(2,1)} async-done(((bf16[2,64,256]{2,0,1:T(2,128)(2,1)}), bf16[2,2048,256]{2,0,1:T(2,128)(2,1)}) %all-gather.7.cloned.1.call-update) | async-done | bytes 2097168 | tf_op jit(solution)/shard_map/all_gather | solution.py:78
  176.1 7.6 %copy.57 = bf16[2,2048,256]{1,0,2:T(2,128)(2,1)S(1)} copy(bf16[2,2048,256]{2,0,1:T(2,128)(2,1)} %all-gather.7.cloned.1.call-done) | data formatting | bytes 4194304 | tf_op jit(solution)/shard_map/all_gather | solution.py:78
  183.6 2.7 gather_fusion
  186.3 1.0 fusion.22
  187.3 1.5 fusion.51
  188.8 0.9 copy.58
  189.7 0.9 copy.59
  190.8 1.6 copy.60
  192.5 3.2 fusion.18
  195.9 0.6 copy-done.8
  196.6 0.8 fusion.16
  197.3 0.7 fusion.21
  198.0 0.3 copy-done.3
  198.4 2.1 fusion.10
  200.6 0.7 convert_element_type.152
  201.3 98.9 %reduce-scatter.3.cloned.1.call-done = bf16[1,512,256]{2,1,0:T(8,128)(2,1)} async-done(((bf16[1,512,2048]{2,1,0:T(8,128)(2,1)}), bf16[1,512,256]{2,1,0:T(8,128)(2,1)}) %reduce-scatter.3.cloned.1.call-update) | async-done | bytes 262160 | tf_op jit(solution)/shard_map/reduce_scatter | solution.py:104
  300.2 1.0 fusion.34
  301.3 1.5 stack.4
  302.8 3.7 all-to-all-start
  306.5 1.6 convert_element_type.154
  308.1 0.2 reduce-scatter.5.cloned.1.call-start
  308.3 113.4 %all-gather.9.cloned.1.call-done = bf16[2,2048,640]{2,1,0:T(8,128)(2,1)} async-done(((bf16[2,64,640]{2,1,0:T(8,128)(2,1)}), bf16[2,2048,640]{2,1,0:T(8,128)(2,1)}) %all-gather.9.cloned.1.call-update) | async-done | bytes 5242896 | tf_op jit(solution)/shard_map/all_gather | solution.py:80
  421.7 5.3 slice_bitcast_fusion.1
  427.1 0.5 multiply_reduce_fusion
  427.6 0.6 bitcast_convert_fusion
  428.3 0.4 fusion.8
  428.7 1.3 copy-done
  430.0 0.8 copy-done.1
  430.8 4.4 fusion
  435.3 78.6 %all-gather.11.cloned.1.call-done = bf16[640,2048]{0,1:T(8,128)(2,1)} async-done(((bf16[640,64]{0,1:T(8,128)(2,1)}), bf16[640,2048]{0,1:T(8,128)(2,1)}) %all-gather.11.cloned.1.call-update) | async-done | bytes 2621456 | tf_op jit(solution)/shard_map/all_gather | solution.py:81
  513.8 5.7 fusion.9
  519.6 0.6 copy-done.10
  521.1 0.8 scatter_fusion
  521.9 0.7 copy.66
  522.6 4.6 all-to-all-start.1
  527.4 14.3 %all-to-all-done.1 = bf16[2,4,128,128]{3,2,0,1:T(8,128)(2,1)S(1)} async-done(((bf16[2,4,128,128]{3,2,0,1:T(8,128)(2,1)}), bf16[2,4,128,128]{3,2,0,1:T(8,128)(2,1)S(1)}, u32[]{:S(2)}, u32[]{:S(2)}) %all-to-all-start.1) | async-done | bytes 262176 | tf_op jit(solution)/shard_map/all_to_all | solution.py:148
  541.7 0.8 scatter_fusion.1
  542.5 72.5 %reduce-scatter.5.cloned.1.call-done = bf16[1,512,256]{2,1,0:T(8,128)(2,1)} async-done(((bf16[1,512,2048]{2,1,0:T(8,128)(2,1)}), bf16[1,512,256]{2,1,0:T(8,128)(2,1)}) %reduce-scatter.5.cloned.1.call-update) | async-done | bytes 262160 | tf_op jit(solution)/shard_map/reduce_scatter | solution.py:120
  615.0 1.7 add_convert_fusion
  (69 shorter events, 2.4 us)
Async XLA Ops:
  7.2 156.9 %all-gather.5.cloned.1.call-start = ((), (), s32[]{:S(2)}) async-start(), calls=%async_computation.4 | async-start | bytes 2359296 | tf_op jit(solution)/shard_map/all_gather | solution.py:87
  7.9 168.2 %all-gather.7.cloned.1.call-start = ((), (), s32[]{:S(2)}) async-start(), calls=%async_computation.5 | async-start | bytes 2162688 | tf_op jit(solution)/shard_map/all_gather | solution.py:78
  9.6 290.6 %reduce-scatter.3.cloned.1.call-start = ((), (), s32[]{:S(2)}) async-start(), calls=%async_computation.6 | async-start | bytes 2359296 | tf_op jit(solution)/shard_map/reduce_scatter | solution.py:104
  188.8 1.7 copy-start.4
  190.8 1.7 copy-start.13
  192.5 3.3 copy-start.11
  192.5 3.3 copy-start.12
  195.6 1.0 copy-start.8
  197.3 1.0 copy-start.3
  198.4 2.2 copy-start.7
  198.4 101.8 %copy-start.2 = (bf16[1,512,256]{2,1,0:T(8,128)(2,1)S(1)}, bf16[1,512,256]{2,1,0:T(8,128)(2,1)}, u32[]{:S(2)}) copy-start(bf16[1,512,256]{2,1,0:T(8,128)(2,1)} %param.12) | copy-start | bytes 786436
  200.5 221.2 %all-gather.9.cloned.1.call-start = ((), (), s32[]{:S(2)}) async-start(), calls=%async_computation.7 | async-start | bytes 5406720 | tf_op jit(solution)/shard_map/all_gather | solution.py:80
  302.8 124.3 %all-to-all-start = ((bf16[8,1,512,256]{2,3,1,0:T(8,128)(2,1)}), bf16[8,1,512,256]{2,3,1,0:T(8,128)(2,1)S(1)}, u32[]{:S(2)}, u32[]{:S(2)}) async-start(bf16[8,1,512,256]{2,3,1,0:T(8,128)(2,1)} %stack.4), calls=%async_computation.1 | async-start | bytes 4194304 | tf_op jit(solution)/shard_map/all_to_all | solution.py:109
  306.5 207.4 %all-gather.11.cloned.1.call-start = ((), (), s32[]{:S(2)}) async-start(), calls=%async_computation.8 | async-start | bytes 2703360 | tf_op jit(solution)/shard_map/all_gather | solution.py:81
  308.1 306.9 %reduce-scatter.5.cloned.1.call-start = ((), (), s32[]{:S(2)}) async-start(), calls=%async_computation.9 | async-start | bytes 2359296 | tf_op jit(solution)/shard_map/reduce_scatter | solution.py:120
  427.6 0.7 copy-start.9
  428.3 1.7 copy-start
  428.3 2.5 copy-start.1
  519.5 0.7 copy-start.10
  520.9 94.1 %copy-start.5 = (bf16[1,512,256]{2,1,0:T(8,128)(2,1)S(1)}, bf16[1,512,256]{2,1,0:T(8,128)(2,1)}, u32[]{:S(2)}) copy-start(bf16[1,512,256]{2,1,0:T(8,128)(2,1)} %reduce-scatter.3.cloned.1.call-done) | copy-start | bytes 786436
  522.6 19.0 %all-to-all-start.1 = ((bf16[2,4,128,128]{3,2,0,1:T(8,128)(2,1)}), bf16[2,4,128,128]{3,2,0,1:T(8,128)(2,1)S(1)}, u32[]{:S(2)}, u32[]{:S(2)}) async-start(bf16[2,4,128,128]{3,2,0,1:T(8,128)(2,1)} %copy.66), calls=%async_computation.3 | async-start | bytes 524288 | tf_op jit(solution)/shard_map/all_to_all | solution.py:148
  542.5 74.3 %copy-start.6 = (bf16[2,4,128,128]{3,2,1,0:T(8,128)(2,1)}, bf16[2,4,128,128]{3,2,1,0:T(8,128)(2,1)S(1)}, u32[]{:S(2)}) copy-start(bf16[2,4,128,128]{3,2,1,0:T(8,128)(2,1)S(1)} %scatter_fusion.1) | copy-start | bytes 786436
Sparse Core Ops, SparseCore 0:
  10.4 74.3 all-gather.4
  87.2 88.8 all-gather.6
  200.6 99.4 reduce-scatter.2
  302.4 119.2 all-gather.8
  424.0 89.8 all-gather.10
  519.7 95.2 reduce-scatter.4
